TPU v7x, 512 devices: a whole 4x8x8 slice. The times are simulated.
512 devices in a mesh: member: 16 (over x_lo, y), dp: 32 (over z, x_hi, core).
Axes of the slice: x: 4 (x_hi: 2, x_lo: 2; x = x_hi * 2 + x_lo), y: 8, z: 8, core: 2. Of those that a mesh axis runs over, the one named last changes fastest.
Arguments:
- inputs: bfloat16 [8192, 64], P('dp'), may hold values from -6 to 6
- observed: float32 [64, 8192], P('member', 'dp'), may hold values from -6 to 6
- noise: bfloat16 [2, 32, 64, 8192], P(None, None, 'member', 'dp'), may hold values from -4 to 4
- w_in: float32 [32, 64, 4096], P('member', None, 'dp'), may hold values from -0.75 to 0.75
- b_in: float32 [32, 4096], P('member', 'dp'), may hold values from -3 to 3
- w_out: float32 [32, 64, 4096], P('member', None, 'dp'), may hold values from -0.09375 to 0.09375
- b_out: float32 [32, 64], P('member'), may hold values from -3 to 3
Outputs:
- new_w_in: float32 [32, 64, 4096], P('member', None, 'dp')
- new_b_in: float32 [32, 4096], P('member', 'dp')
- new_w_out: float32 [32, 64, 4096], P('member', None, 'dp')
- new_b_out: float32 [32, 64], P('member')
All inputs are finite; a program needn't handle non-finite values.
Results may differ from a plain program's by a relative error of at most 0.00056.
Values may be sent and summed in bfloat16 or wider, within the bound.
No kernel may reach another device: no remote copies, remote signals or barrier semaphores. Data moves between devices by JAX's collectives and lax.ppermute only.
A program may use at most 64 MiB of HBM per device.

v0:
```python
import jax
import jax.numpy as jnp
from jax import lax
from jax.sharding import PartitionSpec as P

UPDATES = 2
ridge_level = 0.5


def solve_gain(gram, cross):
    eye = jnp.eye(gram.shape[0], dtype=gram.dtype)
    factor = jnp.linalg.cholesky(gram + ridge_level * eye)
    middle = lax.linalg.triangular_solve(factor, cross, left_side=True, lower=True)
    return lax.linalg.triangular_solve(factor, middle, left_side=True, lower=True, transpose_a=True)


def pack(w_in, b_in, w_out, b_out):
    n = w_in.shape[0]
    return jnp.concatenate(
        [w_in.reshape(n, -1), w_out.reshape(n, -1), b_in.reshape(n, -1), b_out.reshape(n, -1)],
        axis=1,
    )


def unpack(flat, f_in, hid, outs):
    n = flat.shape[0]
    a = f_in * hid
    b = a + outs * hid
    c = b + hid
    return (
        flat[:, :a].reshape(n, f_in, hid),
        flat[:, b:c].reshape(n, hid),
        flat[:, a:b].reshape(n, outs, hid),
        flat[:, c:].reshape(n, outs),
    )


def predict(inputs, own_flat, b_out, f_in, hid, outs):
    n = own_flat.shape[0]
    a = f_in * hid
    b = a + outs * hid
    rounded = own_flat[:, : b + hid].astype(jnp.bfloat16)
    gathered = lax.all_gather(rounded, "dp", axis=0, tiled=False)
    d = gathered.shape[0]
    w_in = gathered[:, :, :a].reshape(d, n, f_in, hid)
    w_out = gathered[:, :, a:b].reshape(d, n, outs, hid)
    b_in = gathered[:, :, b : b + hid]
    pre = jnp.einsum("sf,dnfh->nsdh", inputs, w_in, preferred_element_type=jnp.float32)
    pre = pre + jnp.transpose(b_in, (1, 0, 2)).astype(jnp.float32)[:, None, :, :]
    hidden = jnp.tanh(pre).astype(jnp.bfloat16)
    pred = jnp.einsum("dnoh,nsdh->nos", w_out, hidden, preferred_element_type=jnp.float32)
    return pred + b_out[:, :, None]


def on_device(inputs, observed, noise, w_in, b_in, w_out, b_out):
    per_device = w_in.shape[0]
    f_in, hid = (w_in.shape[1], w_in.shape[2])
    outs = w_out.shape[1]
    count = observed.shape[0] * lax.axis_size("member") * observed.shape[1] * lax.axis_size("dp")
    first = lax.axis_index("member") * per_device
    own = pack(w_in, b_in, w_out, b_out)
    whole = lax.all_gather(own, "member", axis=0, tiled=True)
    for update in range(UPDATES):
        own_b_out = own[:, -outs:]
        predicted = predict(inputs, own, own_b_out, f_in, hid, outs)
        collected = lax.all_to_all(predicted, "member", split_axis=1, concat_axis=0, tiled=True)
        mean_pred = jnp.mean(collected, axis=0)
        anomaly = (collected - mean_pred[None]).reshape(collected.shape[0], -1)
        misfit = (observed[None] + noise[update].astype(jnp.float32) - collected).reshape(
            collected.shape[0], -1
        )
        gram_part = lax.dot_general(
            anomaly, anomaly, (((1,), (1,)), ((), ())), precision=lax.Precision.HIGHEST
        )
        cross_part = lax.dot_general(
            anomaly, misfit, (((1,), (1,)), ((), ())), precision=lax.Precision.HIGHEST
        )
        gram, cross = lax.psum((gram_part, cross_part), ("member", "dp"))
        gain = solve_gain(gram / count, cross / count)
        if update + 1 < UPDATES:
            moved = lax.dot_general(
                gain, whole, (((0,), (0,)), ((), ())), precision=lax.Precision.HIGHEST
            )
            whole = whole + moved
            own = lax.dynamic_slice_in_dim(whole, first, per_device, 0)
        else:
            columns = lax.dynamic_slice_in_dim(gain, first, per_device, 1)
            moved = lax.dot_general(
                columns, whole, (((0,), (0,)), ((), ())), precision=lax.Precision.HIGHEST
            )
            own = own + moved
    return unpack(own, f_in, hid, outs)


def solution(mesh):
    placed = (
        P("dp", None),
        P("member", "dp"),
        P(None, None, "member", "dp"),
        P("member", None, "dp"),
        P("member", "dp"),
        P("member", None, "dp"),
        P("member", None),
    )
    return jax.shard_map(
        on_device,
        mesh=mesh,
        in_specs=placed,
        out_specs=(
            P("member", None, "dp"),
            P("member", "dp"),
            P("member", None, "dp"),
            P("member", None),
        ),
        check_vma=False,
    )
```

profile of v0, /device:TPU:1, one launch (start us, length us, event | category | flops | bytes accessed | tf_op | source)
XLA Modules:
  0.0 511.3 jit_solution(14198276268625181387)
XLA Ops:
  7.2 0.7 convert_bitcast_fusion.2
  7.9 0.8 convert.20
  8.8 0.8 convert.19
  10.4 1.0 copy_bitcast_fusion.2
  11.4 1.4 maximum_bitcast_fusion
  12.8 90.6 %all-gather.7.cloned.1.call-done = bf16[32,2,16512]{2,1,0:T(2,128)(2,1)} async-done(((bf16[1,2,16512]{2,1,0:T(2,128)(2,1)}), bf16[32,2,16512]{2,1,0:T(2,128)(2,1)}) %all-gather.7.cloned.1.call-update) | async-done | bytes 2113552 | tf_op jit(solution)/shard_map/all_gather | solution.py:43
  103.4 0.7 convert_bitcast_fusion.1
  104.1 2.9 fusion.60
  107.1 0.8 reshape.148
  107.9 0.8 reshape.147
  108.8 2.5 fusion.20
  111.3 0.7 copy.43
  112.1 6.6 %all-to-all-start = ((f32[2,64,256]{2,0,1:T(2,128)}), f32[2,64,256]{2,0,1:T(2,128)S(1)}, u32[]{:S(2)}, u32[]{:S(2)}) async-start(f32[2,64,256]{2,0,1:T(2,128)} %copy.43), calls=%async_computation | async-start | bytes 262144 | tf_op jit(solution)/shard_map/all_to_all | solution.py:66
  118.8 47.6 %all-gather.9.cloned.1.call-done = f32[16,2,16576]{2,1,0:T(2,128)} async-done(((f32[1,2,16576]{2,1,0:T(2,128)}), f32[16,2,16576]{2,1,0:T(2,128)}) %all-gather.9.cloned.1.call-update) | async-done | bytes 2121744 | tf_op jit(solution)/shard_map/all_gather | solution.py:62
  166.4 3.7 reshape.128
  170.7 107.1 %all-reduce.1 = (f32[32,32]{0,1:T(8,128)S(1)}, f32[32,32]{0,1:T(8,128)S(1)}) all-reduce(f32[32,32]{0,1:T(8,128)S(1)} %convolution_bitcast_fusion.3, f32[32,32]{0,1:T(8,128)S(1)} %convolution_bitcast_fusion.2), channel_id=1, replica_groups=mesh['member'=16,'dp'=32] {'member','dp'}, use_global_device_ids=true, to_apply=%region_1.0 | all-reduce | flops 2048 | bytes 16384 | tf_op jit(solution)/shard_map/psum | solution.py:78
  277.9 2.9 cholesky.44
  282.1 2.4 custom-call.11
  285.0 4.2 convolution_add_fusion
  289.1 0.7 fusion.35
  289.9 80.4 %all-gather.11.cloned.1.call-done = bf16[32,2,16512]{2,1,0:T(2,128)(2,1)} async-done(((bf16[1,2,16512]{2,1,0:T(2,128)(2,1)}), bf16[32,2,16512]{2,1,0:T(2,128)(2,1)}) %all-gather.11.cloned.1.call-update) | async-done | bytes 2113552 | tf_op jit(solution)/shard_map/all_gather | solution.py:43
  370.3 4.0 fusion.59
  374.4 2.6 reshape.116
  377.0 0.7 convert_bitcast_fusion
  377.8 1.6 reshape.149
  379.4 3.2 fusion.1
  382.6 0.8 fusion.17
  383.6 13.8 %all_to_all.30 = f32[2,64,256]{2,0,1:T(2,128)S(1)} all-to-all(f32[2,64,256]{2,0,1:T(2,128)S(1)} %copy.55), channel_id=1, replica_groups=mesh['member'=16,'dp'=32] {'member'}, dimensions={1} | all-to-all | bytes 262144 | tf_op jit(solution)/shard_map/all_to_all | solution.py:66
  398.0 96.0 %all-reduce = (f32[32,32]{0,1:T(8,128)S(1)}, f32[32,32]{0,1:T(8,128)S(1)}) all-reduce(f32[32,32]{0,1:T(8,128)S(1)} %convolution_bitcast_fusion.1, f32[32,32]{0,1:T(8,128)S(1)} %convolution_bitcast_fusion), channel_id=1, replica_groups=mesh['member'=16,'dp'=32] {'member','dp'}, use_global_device_ids=true, to_apply=%region_6.10 | all-reduce | flops 2048 | bytes 16384 | tf_op jit(solution)/shard_map/psum | solution.py:78
  494.1 2.9 cholesky.55
  498.4 2.4 custom-call.13
  501.3 1.1 convolution_add_fusion.1
  (56 shorter events, 8.5 us)
Async XLA Ops:
  7.2 101.6 %copy-start = (bf16[256,64]{0,1:T(8,128)(2,1)S(1)}, bf16[256,64]{0,1:T(8,128)(2,1)}, u32[]{:S(2)}) copy-start(bf16[256,64]{0,1:T(8,128)(2,1)} %param.12) | copy-start | bytes 98308
  7.2 96.2 %all-gather.7.cloned.1.call-start = ((), (), s32[]{:S(2)}) async-start(), calls=%async_computation.2 | async-start | bytes 2179584 | tf_op jit(solution)/shard_map/all_gather | solution.py:43
  10.3 156.0 %all-gather.9.cloned.1.call-start = ((), (), s32[]{:S(2)}) async-start(), calls=%async_computation.3 | async-start | bytes 2263040 | tf_op jit(solution)/shard_map/all_gather | solution.py:62
  107.1 1.7 copy-start.4
  108.8 9.9 %copy-start.2 = (bf16[2,32,4,256]{3,2,1,0:T(4,128)(2,1)S(1)}, bf16[2,32,4,256]{3,2,1,0:T(4,128)(2,1)}, u32[]{:S(2)}) copy-start(bf16[2,32,4,256]{3,2,1,0:T(4,128)(2,1)} %param.14) | copy-start | bytes 393220
  112.1 58.0 %all-to-all-start = ((f32[2,64,256]{2,0,1:T(2,128)}), f32[2,64,256]{2,0,1:T(2,128)S(1)}, u32[]{:S(2)}, u32[]{:S(2)}) async-start(f32[2,64,256]{2,0,1:T(2,128)} %copy.43), calls=%async_computation | async-start | bytes 262144 | tf_op jit(solution)/shard_map/all_to_all | solution.py:66
  118.6 251.7 %all-gather.11.cloned.1.call-start = ((), (), s32[]{:S(2)}) async-start(), calls=%async_computation.4 | async-start | bytes 2179584 | tf_op jit(solution)/shard_map/all_gather | solution.py:43
  118.7 51.4 %copy-start.3 = (f32[4,256]{1,0:T(4,128)S(1)}, f32[4,256]{1,0:T(4,128)}, u32[]{:S(2)}) copy-start(f32[4,256]{1,0:T(4,128)} %param.13) | copy-start | bytes 12292
  379.4 3.2 copy-start.1
Sparse Core Ops, SparseCore 0:
  11.4 91.9 all-gather.6
  105.5 60.8 all-gather.8
  290.0 80.3 all-gather.10
where the time goes:
time: 512 us; the launch traced here: 511 us
  waiting for transfers between devices  219 us (43%)
  blocking collectives  217 us (42%)
  local copies, waits for them, and re-layouts  21.8 us (4%)
  other arithmetic  19.5 us (4%)
  between operations  14 us (3%)
  matrix products  13.7 us (3%)
  starting transfers between devices  6.69 us (1%)
    psum x2, blocking collectives, on_device(): gram, cross = lax.psum((gram_part, cross_part), ('member', 'dp'))  203 us
    all_gather x2, waiting for transfers between devices, predict(): gathered = lax.all_gather(rounded, 'dp', axis=0, tiled=False)  171 us
    all_gather x1, waiting for transfers between devices, on_device(): whole = lax.all_gather(own, 'member', axis=0, tiled=True)  47.6 us
    all_to_all x1, blocking collectives, on_device(): lax.all_to_all(predicted, 'member', split_axis=1, concat_axis=0, tiled=True)  13.8 us
  transfers between devices with their start and end apart: 4, of which 3 were waited for; matrix products, arithmetic and copies ran while one was open for 3% of the time, Pallas kernels for 0%

commit v1 on v0

--- a/solution.py
+++ b/solution.py
@@ -75,7 +75,7 @@
         cross_part = lax.dot_general(
             anomaly, misfit, (((1,), (1,)), ((), ())), precision=lax.Precision.HIGHEST
         )
-        gram, cross = lax.psum((gram_part, cross_part), ("member", "dp"))
+        gram, cross = lax.psum(lax.psum((gram_part, cross_part), "member"), "dp")
         gain = solve_gain(gram / count, cross / count)
         if update + 1 < UPDATES:
             moved = lax.dot_general(

time: 512 us -> 700 us (1.37)
  blocking collectives: 217 us -> 396 us
    psum x2 -> x4, blocking collectives: 203 us -> 382 us  [on_device(): gram, cross = lax.psum(lax.psum((gram_part, cross_part), 'member'), 'dp')]
  transfers between devices with their start and end apart: 4 -> 4, of which waited for: 3 -> 3; matrix products, arithmetic and copies ran while one was open for 3% -> 2% of each run, Pallas kernels for 0% -> 0%
where the time goes in v1:
time: 700 us; the launch traced here: 695 us
  blocking collectives  396 us (57%)
  waiting for transfers between devices  223 us (32%)
  local copies, waits for them, and re-layouts  21.9 us (3%)
  other arithmetic  19.5 us (3%)
  between operations  14 us (2%)
  matrix products  13.7 us (2%)
    psum x4, blocking collectives, on_device(): gram, cross = lax.psum(lax.psum((gram_part, cross_part), 'member'), 'dp')  382 us
    all_gather x2, waiting for transfers between devices, predict(): gathered = lax.all_gather(rounded, 'dp', axis=0, tiled=False)  176 us
    all_gather x1, waiting for transfers between devices, on_device(): whole = lax.all_gather(own, 'member', axis=0, tiled=True)  47.7 us
  transfers between devices with their start and end apart: 4, of which 3 were waited for; matrix products, arithmetic and copies ran while one was open for 2% of the time, Pallas kernels for 0%

profile of v1, /device:TPU:1, one launch (start us, length us, event | category | flops | bytes accessed | tf_op | source)
XLA Modules:
  0.0 695.3 jit_solution(3234000855787882192)
XLA Ops:
  7.9 0.8 convert.20
  8.8 0.8 convert.19
  10.4 1.0 copy_bitcast_fusion.2
  11.4 1.4 maximum_bitcast_fusion
  12.8 90.6 %all-gather.7.cloned.1.call-done = bf16[32,2,16512]{2,1,0:T(2,128)(2,1)} async-done(((bf16[1,2,16512]{2,1,0:T(2,128)(2,1)}), bf16[32,2,16512]{2,1,0:T(2,128)(2,1)}) %all-gather.7.cloned.1.call-update) | async-done | bytes 2113552 | tf_op jit(solution)/shard_map/all_gather | solution.py:43
  103.4 0.7 convert_bitcast_fusion.1
  104.1 2.9 fusion.60
  107.1 0.8 reshape.148
  107.9 0.8 reshape.147
  108.8 2.5 fusion.20
  111.3 0.8 copy.43
  112.1 6.6 all-to-all-start
  118.8 47.7 %all-gather.9.cloned.1.call-done = f32[16,2,16576]{2,1,0:T(2,128)} async-done(((f32[1,2,16576]{2,1,0:T(2,128)}), f32[16,2,16576]{2,1,0:T(2,128)}) %all-gather.9.cloned.1.call-update) | async-done | bytes 2121744 | tf_op jit(solution)/shard_map/all_gather | solution.py:62
  166.5 3.7 reshape.128
  170.8 48.1 %all-reduce.3 = (f32[32,32]{0,1:T(8,128)S(1)}, f32[32,32]{0,1:T(8,128)S(1)}) all-reduce(f32[32,32]{0,1:T(8,128)S(1)} %convolution_bitcast_fusion.3, f32[32,32]{0,1:T(8,128)S(1)} %convolution_bitcast_fusion.2), channel_id=1, replica_groups=mesh['member'=16,'dp'=32] {'member'}, use_global_device_ids=true, to_apply=%region_1.0 | all-reduce | flops 2048 | bytes 16384 | tf_op jit(solution)/shard_map/psum | solution.py:78
  218.9 148.0 %all-reduce.1 = (f32[32,32]{0,1:T(8,128)S(1)}, f32[32,32]{0,1:T(8,128)S(1)}) all-reduce(f32[32,32]{0,1:T(8,128)S(1)} %get-tuple-element.13, f32[32,32]{0,1:T(8,128)S(1)} %get-tuple-element.14), channel_id=1, replica_groups=mesh['member'=16,'dp'=32] {'dp'}, use_global_device_ids=true, to_apply=%region_2.0 | all-reduce | flops 2048 | bytes 16384 | tf_op jit(solution)/shard_map/psum | solution.py:78
  367.0 2.9 cholesky.44
  371.2 2.4 custom-call.11
  374.1 4.2 convolution_add_fusion
  379.0 85.1 %all-gather.11.cloned.1.call-done = bf16[32,2,16512]{2,1,0:T(2,128)(2,1)} async-done(((bf16[1,2,16512]{2,1,0:T(2,128)(2,1)}), bf16[32,2,16512]{2,1,0:T(2,128)(2,1)}) %all-gather.11.cloned.1.call-update) | async-done | bytes 2113552 | tf_op jit(solution)/shard_map/all_gather | solution.py:43
  464.2 4.1 fusion.59
  468.2 2.6 reshape.116
  470.9 0.7 convert_bitcast_fusion
  471.6 1.6 reshape.149
  473.2 3.2 fusion.1
  476.5 0.8 fusion.17
  477.4 13.8 %all_to_all.30 = f32[2,64,256]{2,0,1:T(2,128)S(1)} all-to-all(f32[2,64,256]{2,0,1:T(2,128)S(1)} %copy.55), channel_id=1, replica_groups=mesh['member'=16,'dp'=32] {'member'}, dimensions={1} | all-to-all | bytes 262144 | tf_op jit(solution)/shard_map/all_to_all | solution.py:66
  491.9 47.7 %all-reduce.2 = (f32[32,32]{0,1:T(8,128)S(1)}, f32[32,32]{0,1:T(8,128)S(1)}) all-reduce(f32[32,32]{0,1:T(8,128)S(1)} %convolution_bitcast_fusion.1, f32[32,32]{0,1:T(8,128)S(1)} %convolution_bitcast_fusion), channel_id=1, replica_groups=mesh['member'=16,'dp'=32] {'member'}, use_global_device_ids=true, to_apply=%region_8.12 | all-reduce | flops 2048 | bytes 16384 | tf_op jit(solution)/shard_map/psum | solution.py:78
  539.6 138.4 %all-reduce = (f32[32,32]{0,1:T(8,128)S(1)}, f32[32,32]{0,1:T(8,128)S(1)}) all-reduce(f32[32,32]{0,1:T(8,128)S(1)} %get-tuple-element.11, f32[32,32]{0,1:T(8,128)S(1)} %get-tuple-element.12), channel_id=1, replica_groups=mesh['member'=16,'dp'=32] {'dp'}, use_global_device_ids=true, to_apply=%region_9.13 | all-reduce | flops 2048 | bytes 16384 | tf_op jit(solution)/shard_map/psum | solution.py:78
  678.1 2.9 cholesky.55
  682.3 2.4 custom-call.13
  685.2 1.1 convolution_add_fusion.1
  (58 shorter events, 9.9 us)
Async XLA Ops:
  7.2 101.6 %copy-start = (bf16[256,64]{0,1:T(8,128)(2,1)S(1)}, bf16[256,64]{0,1:T(8,128)(2,1)}, u32[]{:S(2)}) copy-start(bf16[256,64]{0,1:T(8,128)(2,1)} %param.12) | copy-start | bytes 98308
  7.2 96.2 %all-gather.7.cloned.1.call-start = ((), (), s32[]{:S(2)}) async-start(), calls=%async_computation.2 | async-start | bytes 2179584 | tf_op jit(solution)/shard_map/all_gather | solution.py:43
  10.3 156.1 %all-gather.9.cloned.1.call-start = ((), (), s32[]{:S(2)}) async-start(), calls=%async_computation.3 | async-start | bytes 2263040 | tf_op jit(solution)/shard_map/all_gather | solution.py:62
  107.1 1.7 copy-start.4
  108.8 9.9 %copy-start.2 = (bf16[2,32,4,256]{3,2,1,0:T(4,128)(2,1)S(1)}, bf16[2,32,4,256]{3,2,1,0:T(4,128)(2,1)}, u32[]{:S(2)}) copy-start(bf16[2,32,4,256]{3,2,1,0:T(4,128)(2,1)} %param.14) | copy-start | bytes 393220
  112.1 58.1 %all-to-all-start = ((f32[2,64,256]{2,0,1:T(2,128)}), f32[2,64,256]{2,0,1:T(2,128)S(1)}, u32[]{:S(2)}, u32[]{:S(2)}) async-start(f32[2,64,256]{2,0,1:T(2,128)} %copy.43), calls=%async_computation | async-start | bytes 262144 | tf_op jit(solution)/shard_map/all_to_all | solution.py:66
  118.6 345.5 %all-gather.11.cloned.1.call-start = ((), (), s32[]{:S(2)}) async-start(), calls=%async_computation.4 | async-start | bytes 2179584 | tf_op jit(solution)/shard_map/all_gather | solution.py:43
  118.8 51.5 %copy-start.3 = (f32[4,256]{1,0:T(4,128)S(1)}, f32[4,256]{1,0:T(4,128)}, u32[]{:S(2)}) copy-start(f32[4,256]{1,0:T(4,128)} %param.13) | copy-start | bytes 12292
  473.2 3.2 copy-start.1
Sparse Core Ops, SparseCore 0:
  11.4 91.9 all-gather.6
  105.5 60.9 all-gather.8
  379.1 85.0 all-gather.10
